TPU v7x, 256 devices: a whole 4x4x8 slice. The times are simulated.
256 devices in a mesh: col: 64 (over x, z, core), row: 4 (over y).
Axes of the slice: x: 4, y: 4, z: 8, core: 2. Of those that a mesh axis runs over, the one named last changes fastest.
Arguments:
- matrix: float32 [16, 4, 256, 1, 64, 256], P(None, 'row', None, None, 'col'), as said below
Outputs:
- factored: float32 [16, 4, 256, 1, 64, 256], P(None, 'row', None, None, 'col')
Inputs may be any that keep to these rules, and one draw needn't show every extreme that they name: matrix is symmetric and positive definite, a Matern covariance of spatial sites plus a symmetric measurement term and a nugget.
All inputs are finite; a program needn't handle non-finite values.
Results may differ from a plain program's by a relative error of at most 0.0003.
Values sent between devices are 32-bit elements; how exact they have to be, the bound alone decides.
No kernel may reach another device: no remote copies, remote signals or barrier semaphores. Data moves between devices by JAX's collectives and lax.ppermute only.
A program may use at most 128 MiB of HBM per device.

v0:
```python
import jax
import jax.numpy as jnp
from jax import lax
from jax.sharding import PartitionSpec as P

STEPS = 3
HI = lax.Precision.HIGHEST


def mm_hi(a, b):
    return jnp.einsum(
        "...ps,qs->...pq", a, b, precision=HI, preferred_element_type=jnp.float32
    )


def mm_lo(a, b):
    return jnp.einsum(
        "...ps,qs->...pq",
        a.astype(jnp.bfloat16),
        b.astype(jnp.bfloat16),
        preferred_element_type=jnp.float32,
    )


def factor(tile, eye):
    low = jnp.linalg.cholesky(tile)
    inverse = lax.linalg.triangular_solve(low, eye, left_side=True, lower=True)
    return low, inverse


def on_device(matrix):
    tile_rows = matrix.shape[0]
    width = matrix.shape[2]
    n_row = lax.axis_size("row")
    n_col = lax.axis_size("col")
    quarter = width // n_row
    my_row = lax.axis_index("row")
    my_col = lax.axis_index("col")
    tiles = matrix.reshape(tile_rows, width, width)
    eye = jnp.eye(width, dtype=jnp.float32)

    head = lax.all_gather(tiles[0], "row", axis=0, tiled=False)

    cols = lax.dynamic_slice_in_dim(head[:STEPS], my_row * quarter, quarter, axis=2)
    piece = jnp.swapaxes(cols, 1, 2)
    perm = []
    for c in range(n_col):
        for r in range(n_row):
            dst_col = c - c % n_row + r
            perm.append((c * n_row + r, dst_col * n_row + c % n_row))
    piece = lax.ppermute(piece, ("col", "row"), perm)

    gathered = lax.all_gather(piece, "col", axis=1, tiled=False)
    raw = gathered.reshape(STEPS, tile_rows, width, width)

    source = [(my_row + k) % STEPS for k in range(2)]
    share = jnp.stack([jnp.where(my_col == s, tiles[0], 0.0) for s in source])
    span = 1
    while span < n_col:
        moved = lax.ppermute(share, "col", [(i, (i + span) % n_col) for i in range(n_col)])
        held = jnp.stack([(my_col - s) % n_col < span for s in source])
        share = jnp.where(held[:, None, None], share, moved)
        span *= 2
    shares = [share] + [
        lax.ppermute(share, "row", [(i, (i + d) % n_row) for i in range(n_row)])
        for d in range(1, n_row)
    ]
    shares = jnp.stack(shares)

    def lead(group, k):
        from_group = lax.dynamic_index_in_dim(shares, (my_row - group) % n_row, 0, keepdims=False)
        return from_group[k]

    a00 = lead(0, 0)
    a10 = lead(0, 1).T
    a11 = lead(1, 0)
    a21 = lead(1, 1).T
    a22 = lead(2, 0)
    a20 = lead(2, 1)

    l0, i0 = factor(a00, eye)
    p01 = mm_hi(a10, i0)
    p02 = mm_hi(a20, i0)
    b11 = a11 - mm_hi(p01, p01)
    b21 = a21 - mm_hi(p02, p01)
    b22 = a22 - mm_hi(p02, p02)
    l1, i1 = factor(b11, eye)
    p12 = mm_hi(b21, i1)
    c22 = b22 - mm_hi(p12, p12)
    l2, i2 = factor(c22, eye)

    def sub(step, target, low_rows, partner, exact_rows):
        lo = mm_lo(low_rows, partner)
        hi = mm_hi(exact_rows, partner)
        t0 = my_row
        exact = (t0 == step) | (t0 == step + 1)
        first = jnp.where(exact, hi, lo[0])
        return target - lo.at[0].set(first)

    q0 = mm_hi(raw[0], i0)
    m1 = sub(1, raw[1], q0, p01, q0[0])
    q1 = mm_hi(m1, i1)
    m2 = sub(2, raw[2], q0, p02, q0[0])
    m2 = sub(2, m2, q1, p12, q1[0])
    q2 = mm_hi(m2, i2)

    own = jnp.swapaxes(head[:STEPS], 1, 2)
    c = my_col

    def own_sub(step, target, rows, partner):
        exact = (c == step) | (c == step + 1)
        return target - jnp.where(exact, mm_hi(rows, partner), mm_lo(rows, partner))

    r0 = mm_hi(own[0], i0)
    r1 = mm_hi(own_sub(1, own[1], r0, p01), i1)
    r2 = mm_hi(own_sub(2, own_sub(2, own[2], r0, p02), r1, p12), i2)

    rows_cat = jnp.concatenate([q0, q1, q2], axis=-1)
    col_cat = jnp.concatenate([r0, r1, r2], axis=-1)
    update = mm_lo(rows_cat, col_cat)
    offset = (my_row - c) % n_row
    near = c + offset
    local = jnp.clip((near - my_row) // n_row, 0, tile_rows - 1)
    valid = (offset <= 1) & (near < tile_rows * n_row)
    exact = mm_hi(lax.dynamic_index_in_dim(rows_cat, local, 0, keepdims=False), col_cat)
    before = lax.dynamic_index_in_dim(update, local, 0, keepdims=False)
    chosen = jnp.where(valid, exact, before)
    update = lax.dynamic_update_index_in_dim(update, chosen, local, 0)

    row_ids = (jnp.arange(tile_rows, dtype=jnp.int32) * n_row + my_row)[:, None, None]
    trailing = jnp.where(row_ids >= c, tiles - update, tiles)
    panel = jnp.where(c == 0, q0, jnp.where(c == 1, q1, q2))
    diag = jnp.where(c == 0, l0, jnp.where(c == 1, l1, l2))
    leading = jnp.where(row_ids > c, panel, jnp.where(row_ids == c, diag[None], tiles))
    out = jnp.where(c >= STEPS, trailing, leading)
    return out.reshape(matrix.shape)


def solution(mesh):
    placed = (P(None, "row", None, None, "col", None),)
    return jax.shard_map(
        on_device,
        mesh=mesh,
        in_specs=placed,
        out_specs=P(None, "row", None, None, "col", None),
        check_vma=False,
    )
```

profile of v0, /device:TPU:16, one launch (start us, length us, event | category | flops | bytes accessed | tf_op | source)
XLA Modules:
  0.0 496.6 jit_solution(14492754272435557581)
XLA Ops:
  8.5 29.2 %all-gather.5.cloned.1.call-done = f32[4,1,256,1,1,256]{5,2,4,3,1,0:T(8,128)} async-done(((f32[1,1,256,1,1,256]{5,2,4,3,1,0:T(8,128)}), f32[4,1,256,1,1,256]{5,2,4,3,1,0:T(8,128)}) %all-gather.5.cloned.1.call-update) | async-done | bytes 1048592 | tf_op jit(solution)/shard_map/all_gather | solution.py:42
  43.6 6.6 %collective-permute-done = f32[3,64,256]{2,1,0:T(8,128)S(1)} collective-permute-done((f32[3,64,256]{2,1,0:T(8,128)S(1)}, f32[3,64,256]{2,1,0:T(8,128)S(1)}, u32[]{:S(2)}, u32[]{:S(2)}) %collective-permute-start) | collective-permute-done | bytes 196640 | tf_op jit(solution)/shard_map/ppermute | solution.py:51
  51.4 11.8 %collective-permute-done.1 = f32[2,256,256]{1,2,0:T(8,128)S(1)} collective-permute-done((f32[2,256,256]{1,2,0:T(8,128)S(1)}, f32[2,256,256]{1,2,0:T(8,128)S(1)}, u32[]{:S(2)}, u32[]{:S(2)}) %collective-permute-start.1) | collective-permute-done | bytes 524320 | tf_op jit(solution)/shard_map/ppermute | solution.py:60
  63.5 17.1 %collective-permute-done.2 = f32[2,256,256]{1,2,0:T(8,128)S(1)} collective-permute-done((f32[2,256,256]{1,2,0:T(8,128)S(1)}, f32[2,256,256]{1,2,0:T(8,128)S(1)}, u32[]{:S(2)}, u32[]{:S(2)}) %collective-permute-start.2) | collective-permute-done | bytes 524320 | tf_op jit(solution)/shard_map/ppermute | solution.py:60
  81.0 24.3 %collective-permute-done.3 = f32[2,256,256]{1,2,0:T(8,128)S(1)} collective-permute-done((f32[2,256,256]{1,2,0:T(8,128)S(1)}, f32[2,256,256]{1,2,0:T(8,128)S(1)}, u32[]{:S(2)}, u32[]{:S(2)}) %collective-permute-start.3) | collective-permute-done | bytes 524320 | tf_op jit(solution)/shard_map/ppermute | solution.py:60
  105.5 36.2 %collective-permute-done.4 = f32[2,256,256]{1,2,0:T(8,128)S(1)} collective-permute-done((f32[2,256,256]{1,2,0:T(8,128)S(1)}, f32[2,256,256]{1,2,0:T(8,128)S(1)}, u32[]{:S(2)}, u32[]{:S(2)}) %collective-permute-start.4) | collective-permute-done | bytes 524320 | tf_op jit(solution)/shard_map/ppermute | solution.py:60
  142.0 19.3 %collective-permute-done.5 = f32[2,256,256]{1,2,0:T(8,128)S(1)} collective-permute-done((f32[2,256,256]{1,2,0:T(8,128)S(1)}, f32[2,256,256]{1,2,0:T(8,128)S(1)}, u32[]{:S(2)}, u32[]{:S(2)}) %collective-permute-start.5) | collective-permute-done | bytes 524320 | tf_op jit(solution)/shard_map/ppermute | solution.py:60
  161.7 12.6 %collective-permute-done.6 = f32[2,256,256]{1,2,0:T(8,128)S(1)} collective-permute-done((f32[2,256,256]{1,2,0:T(8,128)S(1)}, f32[2,256,256]{1,2,0:T(8,128)S(1)}, u32[]{:S(2)}, u32[]{:S(2)}) %collective-permute-start.6) | collective-permute-done | bytes 524320 | tf_op jit(solution)/shard_map/ppermute | solution.py:60
  175.3 8.6 %collective-permute-start.8 = (f32[2,256,256]{1,2,0:T(8,128)S(1)}, f32[2,256,256]{1,2,0:T(8,128)S(1)}, u32[]{:S(2)}, u32[]{:S(2)}) collective-permute-start(f32[2,256,256]{1,2,0:T(8,128)S(1)} %broadcast_select_fusion.5), channel_id=1, source_target_pairs={{0,2},{1,3},{2,0},{3,1},{4,6},{5,7},{6,4},{7,5},{8,10},{9,11},{10,... | collective-permute-start | bytes 1572872 | tf_op jit(solution)/shard_map/ppermute | solution.py:65
  186.6 10.9 %copy.39 = f32[16,1,256,1,1,256]{2,5,0,4,3,1:T(8,128)} copy(f32[16,1,256,1,1,256]{5,4,3,2,1,0:T(1,128)} %param.10) | data formatting | bytes 8388608 | tf_op args[0]
  197.6 7.9 %collective-permute-done.8 = f32[2,256,256]{1,2,0:T(8,128)S(1)} collective-permute-done((f32[2,256,256]{1,2,0:T(8,128)S(1)}, f32[2,256,256]{1,2,0:T(8,128)S(1)}, u32[]{:S(2)}, u32[]{:S(2)}) %collective-permute-start.8) | collective-permute-done | bytes 524320 | tf_op jit(solution)/shard_map/ppermute | solution.py:65
  209.0 11.7 %cholesky.172 = f32[128,128]{1,0:T(8,128)S(1)} custom-call(f32[128,128]{1,0:T(8,128)S(1)} %cholesky.270), custom_call_target="Cholesky" | custom-call | tf_op jit(solution)/shard_map/jit(cholesky)/cholesky | solution.py:26
  220.8 9.8 %custom-call.15 = f32[1,128,128]{1,2,0:T(8,128)S(1)} custom-call(f32[1,128,128]{2,1,0:T(8,128)S(1)} %get-tuple-element.114), custom_call_target="InvertDiagBlocksLowerTriangular" | custom-call | tf_op jit(solution)/shard_map/jit(cholesky)/cholesky | solution.py:26
  231.1 11.7 %cholesky.189 = f32[128,128]{1,0:T(8,128)S(1)} custom-call(f32[128,128]{1,0:T(8,128)S(1)} %convolution_subtract_fusion.5), custom_call_target="Cholesky" | custom-call | tf_op jit(solution)/shard_map/jit(cholesky)/cholesky | solution.py:26
  249.7 20.1 %custom-call.16 = f32[2,128,128]{1,2,0:T(8,128)S(1)} custom-call(f32[2,128,128]{2,1,0:T(8,128)S(1)} %get-tuple-element.63), custom_call_target="InvertDiagBlocksLowerTriangular" | custom-call | tf_op jit(solution)/shard_map/triangular_solve/custom-call.0 | solution.py:27
  274.1 11.7 %cholesky.206 = f32[128,128]{1,0:T(8,128)S(1)} custom-call(f32[128,128]{1,0:T(8,128)S(1)} %cholesky.273), custom_call_target="Cholesky" | custom-call | tf_op jit(solution)/shard_map/jit(cholesky)/cholesky | solution.py:26
  285.9 10.4 %custom-call.17 = f32[1,128,128]{1,2,0:T(8,128)} custom-call(f32[1,128,128]{2,1,0:T(8,128)S(1)} %get-tuple-element.110), custom_call_target="InvertDiagBlocksLowerTriangular" | custom-call | tf_op jit(solution)/shard_map/jit(cholesky)/cholesky | solution.py:26
  298.5 11.7 %cholesky.223 = f32[128,128]{1,0:T(8,128)S(1)} custom-call(f32[128,128]{1,0:T(8,128)S(1)} %convolution_subtract_fusion.4), custom_call_target="Cholesky" | custom-call | tf_op jit(solution)/shard_map/jit(cholesky)/cholesky | solution.py:26
  313.6 7.0 %while.10 = (s32[]{:T(128)}, f32[256,256]{1,0:T(8,128)}, s32[2,2]{1,0:T(2,128)}, f32[2,128,128]{2,1,0:T(8,128)S(1)}, s32[]{:T(128)}) while((s32[]{:T(128)}, f32[256,256]{1,0:T(8,128)}, s32[2,2]{1,0:T(2,128)}, f32[2,128,128]{2,1,0:T(8,128)S(1)}, s32[]{:T(128)}) %tuple.90), condition=%wide.while_cond.3.clone, body=%wide.while_body.3.clone.sunk | while | flops 2 | bytes 131181 | solution.py:27
  320.6 20.4 %custom-call.18 = f32[2,128,128]{1,2,0:T(8,128)} custom-call(f32[2,128,128]{2,1,0:T(8,128)S(1)} %get-tuple-element.64), custom_call_target="InvertDiagBlocksLowerTriangular" | custom-call | tf_op jit(solution)/shard_map/triangular_solve/custom-call.0 | solution.py:27
  349.7 11.7 %cholesky.240 = f32[128,128]{1,0:T(8,128)S(1)} custom-call(f32[128,128]{1,0:T(8,128)S(1)} %cholesky.276), custom_call_target="Cholesky" | custom-call | tf_op jit(solution)/shard_map/jit(cholesky)/cholesky | solution.py:26
  361.5 9.8 %custom-call.19 = f32[1,128,128]{1,2,0:T(8,128)S(1)} custom-call(f32[1,128,128]{2,1,0:T(8,128)S(1)} %get-tuple-element.106), custom_call_target="InvertDiagBlocksLowerTriangular" | custom-call | tf_op jit(solution)/shard_map/jit(cholesky)/cholesky | solution.py:26
  371.8 11.9 %cholesky.257 = f32[128,128]{1,0:T(8,128)S(1)} custom-call(f32[128,128]{1,0:T(8,128)S(1)} %convolution_subtract_fusion.3), custom_call_target="Cholesky" | custom-call | tf_op jit(solution)/shard_map/jit(cholesky)/cholesky | solution.py:26
  391.6 19.7 %custom-call.20 = f32[2,128,128]{1,2,0:T(8,128)S(1)} custom-call(f32[2,128,128]{2,1,0:T(8,128)S(1)} %get-tuple-element.65), custom_call_target="InvertDiagBlocksLowerTriangular" | custom-call | tf_op jit(solution)/shard_map/triangular_solve/custom-call.0 | solution.py:27
  417.1 9.5 %fusion.110 = (f32[1,4096,256]{2,1,0:T(8,128)}, f32[1,4096,256]{2,1,0:T(8,128)}, f32[1,4096,256]{2,1,0:T(8,128)}) fusion(f32[3,4096,256]{2,1,0:T(8,128)} %all-gather.7.cloned.1.call-done), kind=kLoop, calls=%fused_computation.206 | loop fusion | bytes 25165824 | tf_op jit(solution)/shard_map/slice | solution.py:103
  426.6 6.1 %fusion.46 = f32[16,256,256]{1,2,0:T(8,128)S(1)} fusion(f32[16,256,256]{2,1,0:T(8,128)} %bitcast.272, f32[128,256]{1,0:T(8,128)S(1)} %fusion.74, f32[128,256]{1,0:T(8,128)S(1)} %fusion.63), kind=kOutput, calls=%fused_computation.88 | convolution fusion | flops 3221291008 | bytes 8650752 | tf_op jit(solution)/shard_map/...ps,qs->...pq/dot_general | solution.py:11
  436.3 4.5 fusion.8
  444.5 4.7 fusion.5
  449.3 5.6 %pad_maximum_fusion = f32[16,256,768]{1,2,0:T(8,128)} fusion(f32[16,256,256]{1,2,0:T(8,128)S(1)} %fusion.5, f32[16,256,256]{1,2,0:T(8,128)S(1)} %fusion.8, f32[16,256,256]{1,2,0:T(8,128)S(1)} %fusion.46), kind=kLoop, calls=%fused_computation.6 | loop fusion | flops 6291456 | bytes 25165824 | tf_op jit(solution)/shard_map/concatenate | solution.py:118
  458.6 5.4 %copy.56 = f32[16,256,256]{1,2,0:T(8,128)} copy(f32[16,256,256]{2,1,0:T(8,128)} %fusion) | data formatting | bytes 8388608 | tf_op jit(solution)/shard_map/...ps,qs->...pq/dot_general | solution.py:17
  468.3 10.4 %fusion.3 = f32[16,1,256,1,1,256]{2,5,0,4,3,1:T(8,128)} fusion(f32[16,256,256]{1,2,0:T(8,128)} %fusion.22, f32[16,1,256,1,1,256]{2,5,0,4,3,1:T(8,128)} %copy.39, f32[16,256,256]{1,2,0:T(8,128)} %copy-done, f32[16,256,256]{1,2,0:T(8,128)} %copy-done.1, f32[16,256,256]{1,2,0:T(8,128)} %copy-done.2, f32[256,256]{0,1:T(8,128)S(1)} %copy.57, ...), kind=kLoop, calls=%fused_computation.11 | loop fusion | flops 7340032 | bytes 25428020 | tf_op jit(solution)/shard_map/reshape | solution.py:136
  478.7 10.9 %copy.58 = f32[16,1,256,1,1,256]{5,4,3,2,1,0:T(1,128)} copy(f32[16,1,256,1,1,256]{2,5,0,4,3,1:T(8,128)} %fusion.3) | data formatting | bytes 8388608 | tf_op jit(solution)/shard_map/reshape | solution.py:136
  (173 shorter events, 84.0 us)
Async XLA Ops:
  6.5 31.2 %all-gather.5.cloned.1.call-start = ((), (), s32[]{:S(2)}) async-start(), calls=%async_computation | async-start | bytes 1310720 | tf_op jit(solution)/shard_map/all_gather | solution.py:42
  8.4 408.7 %all-gather.7.cloned.1.call-start = ((), (), s32[]{:S(2)}) async-start(), calls=%async_computation.1 | async-start | bytes 12779520 | tf_op jit(solution)/shard_map/all_gather | solution.py:53
  39.2 11.9 %copy-start.5 = (f32[3,1,256,1,1,256]{2,5,0,4,3,1:T(8,128)}, f32[3,1,256,1,1,256]{2,5,0,4,3,1:T(8,128)S(1)}, u32[]{:S(2)}) copy-start(f32[3,1,256,1,1,256]{2,5,0,4,3,1:T(8,128)S(1)} %copy.70) | copy-start | bytes 2359300
  39.2 11.0 %collective-permute-start = (f32[3,64,256]{2,1,0:T(8,128)S(1)}, f32[3,64,256]{2,1,0:T(8,128)S(1)}, u32[]{:S(2)}, u32[]{:S(2)}) collective-permute-start(f32[3,64,256]{2,1,0:T(8,128)S(1)} %dynamic-slice_bitcast_fusion.8), channel_id=1, source_target_pairs={{0,0},{1,4},{2,8},{3,12},{4,1},{5,5},{6,9},{7,13},{8,2},{9,6},{10,... | collective-permute-start | bytes 589832 | tf_op jit(solution)/shard_map/ppermute | solution.py:51
  50.2 0.7 copy-start.15
  51.2 12.0 %collective-permute-start.1 = (f32[2,256,256]{1,2,0:T(8,128)S(1)}, f32[2,256,256]{1,2,0:T(8,128)S(1)}, u32[]{:S(2)}, u32[]{:S(2)}) collective-permute-start(f32[2,256,256]{1,2,0:T(8,128)S(1)} %pad_maximum_fusion.4), channel_id=1, source_target_pairs={{0,4},{4,8},{8,12},{12,16},{16,20},{20,24},{24,28},{28,32},{32,36}... | collective-permute-start | bytes 1572872 | tf_op jit(solution)/shard_map/ppermute | solution.py:60
  63.3 17.3 %collective-permute-start.2 = (f32[2,256,256]{1,2,0:T(8,128)S(1)}, f32[2,256,256]{1,2,0:T(8,128)S(1)}, u32[]{:S(2)}, u32[]{:S(2)}) collective-permute-start(f32[2,256,256]{1,2,0:T(8,128)S(1)} %broadcast_select_fusion), channel_id=1, source_target_pairs={{0,8},{4,12},{8,16},{12,20},{16,24},{20,28},{24,32},{28,36},{32,40... | collective-permute-start | bytes 1572872 | tf_op jit(solution)/shard_map/ppermute | solution.py:60
  80.8 24.4 %collective-permute-start.3 = (f32[2,256,256]{1,2,0:T(8,128)S(1)}, f32[2,256,256]{1,2,0:T(8,128)S(1)}, u32[]{:S(2)}, u32[]{:S(2)}) collective-permute-start(f32[2,256,256]{1,2,0:T(8,128)S(1)} %broadcast_select_fusion.1), channel_id=1, source_target_pairs={{0,16},{4,20},{8,24},{12,28},{16,32},{20,36},{24,40},{28,44},{32,4... | collective-permute-start | bytes 1572872 | tf_op jit(solution)/shard_map/ppermute | solution.py:60
  105.4 36.4 %collective-permute-start.4 = (f32[2,256,256]{1,2,0:T(8,128)S(1)}, f32[2,256,256]{1,2,0:T(8,128)S(1)}, u32[]{:S(2)}, u32[]{:S(2)}) collective-permute-start(f32[2,256,256]{1,2,0:T(8,128)S(1)} %broadcast_select_fusion.2), channel_id=1, source_target_pairs={{0,32},{4,36},{8,40},{12,44},{16,48},{20,52},{24,56},{28,60},{32,6... | collective-permute-start | bytes 1572872 | tf_op jit(solution)/shard_map/ppermute | solution.py:60
  141.9 19.5 %collective-permute-start.5 = (f32[2,256,256]{1,2,0:T(8,128)S(1)}, f32[2,256,256]{1,2,0:T(8,128)S(1)}, u32[]{:S(2)}, u32[]{:S(2)}) collective-permute-start(f32[2,256,256]{1,2,0:T(8,128)S(1)} %broadcast_select_fusion.3), channel_id=1, source_target_pairs={{0,64},{4,68},{8,72},{12,76},{16,80},{20,84},{24,88},{28,92},{32,9... | collective-permute-start | bytes 1572872 | tf_op jit(solution)/shard_map/ppermute | solution.py:60
  161.5 12.7 %collective-permute-start.6 = (f32[2,256,256]{1,2,0:T(8,128)S(1)}, f32[2,256,256]{1,2,0:T(8,128)S(1)}, u32[]{:S(2)}, u32[]{:S(2)}) collective-permute-start(f32[2,256,256]{1,2,0:T(8,128)S(1)} %broadcast_select_fusion.4), channel_id=1, source_target_pairs={{0,128},{4,132},{8,136},{12,140},{16,144},{20,148},{24,152},{28,15... | collective-permute-start | bytes 1572872 | tf_op jit(solution)/shard_map/ppermute | solution.py:60
  174.4 23.2 %copy-start.11 = (f32[2,256,256]{1,2,0:T(8,128)}, f32[2,256,256]{1,2,0:T(8,128)S(1)}, u32[]{:S(2)}) copy-start(f32[2,256,256]{1,2,0:T(8,128)S(1)} %broadcast_select_fusion.5) | copy-start | bytes 1572868
  174.4 23.2 %collective-permute-start.7 = (f32[2,256,256]{1,2,0:T(8,128)S(1)}, f32[2,256,256]{1,2,0:T(8,128)S(1)}, u32[]{:S(2)}, u32[]{:S(2)}) collective-permute-start(f32[2,256,256]{1,2,0:T(8,128)S(1)} %broadcast_select_fusion.5), channel_id=1, source_target_pairs={{0,1},{1,2},{2,3},{3,0},{4,5},{5,6},{6,7},{7,4},{8,9},{9,10},{10,1... | collective-permute-start | bytes 1572872 | tf_op jit(solution)/shard_map/ppermute | solution.py:65
  175.3 30.2 %collective-permute-start.8 = (f32[2,256,256]{1,2,0:T(8,128)S(1)}, f32[2,256,256]{1,2,0:T(8,128)S(1)}, u32[]{:S(2)}, u32[]{:S(2)}) collective-permute-start(f32[2,256,256]{1,2,0:T(8,128)S(1)} %broadcast_select_fusion.5), channel_id=1, source_target_pairs={{0,2},{1,3},{2,0},{3,1},{4,6},{5,7},{6,4},{7,5},{8,10},{9,11},{10,... | collective-permute-start | bytes 1572872 | tf_op jit(solution)/shard_map/ppermute | solution.py:65
  183.9 22.5 %collective-permute-start.9 = (f32[2,256,256]{1,2,0:T(8,128)S(1)}, f32[2,256,256]{1,2,0:T(8,128)S(1)}, u32[]{:S(2)}, u32[]{:S(2)}) collective-permute-start(f32[2,256,256]{1,2,0:T(8,128)S(1)} %broadcast_select_fusion.5), channel_id=1, source_target_pairs={{0,3},{1,0},{2,1},{3,2},{4,7},{5,4},{6,5},{7,6},{8,11},{9,8},{10,9... | collective-permute-start | bytes 1572872 | tf_op jit(solution)/shard_map/ppermute | solution.py:65
  205.5 0.9 copy-start.13
  206.4 0.8 copy-start.14
  242.8 70.8 %copy-start.7 = (f32[256,256]{1,0:T(8,128)}, f32[256,256]{1,0:T(8,128)S(1)}, u32[]{:S(2)}) copy-start(f32[256,256]{1,0:T(8,128)S(1)} %get-tuple-element.112) | copy-start | bytes 786436
  249.1 0.6 copy-start.16
  273.4 0.7 copy-start.12
  310.2 34.8 %copy-start.8 = (f32[256,256]{1,0:T(8,128)}, f32[256,256]{1,0:T(8,128)S(1)}, u32[]{:S(2)}) copy-start(f32[256,256]{1,0:T(8,128)S(1)} %get-tuple-element.108) | copy-start | bytes 786436
  343.9 43.5 %copy-start.17 = (s32[2,2]{1,0:T(2,128)S(1)}, s32[2,2]{1,0:T(2,128)}, u32[]{:S(2)}) copy-start(s32[2,2]{1,0:T(2,128)} %get-tuple-element.289) | copy-start | bytes 52
  345.1 1.3 copy-start.9
  347.5 66.8 %copy-start.6 = (f32[3,1,256,1,1,256]{2,5,0,4,3,1:T(8,128)S(1)}, f32[3,1,256,1,1,256]{2,5,0,4,3,1:T(8,128)}, u32[]{:S(2)}) copy-start(f32[3,1,256,1,1,256]{2,5,0,4,3,1:T(8,128)} %copy-done.5) | copy-start | bytes 2359300
  349.7 64.9 %copy-start.10 = (f32[128,256]{1,0:T(8,128)S(1)}, f32[128,256]{1,0:T(8,128)}, u32[]{:S(2)}) copy-start(f32[128,256]{1,0:T(8,128)} %copy-done.9) | copy-start | bytes 393220
  432.7 22.3 %copy-start = (f32[16,256,256]{1,2,0:T(8,128)}, f32[16,256,256]{1,2,0:T(8,128)S(1)}, u32[]{:S(2)}) copy-start(f32[16,256,256]{1,2,0:T(8,128)S(1)} %fusion.46) | copy-start | bytes 12582916
  433.5 2.9 copy-start.3
  440.8 14.1 %copy-start.1 = (f32[16,256,256]{1,2,0:T(8,128)}, f32[16,256,256]{1,2,0:T(8,128)S(1)}, u32[]{:S(2)}) copy-start(f32[16,256,256]{1,2,0:T(8,128)S(1)} %fusion.8) | copy-start | bytes 12582916
  440.8 3.7 copy-start.4
  449.3 5.8 %copy-start.2 = (f32[16,256,256]{1,2,0:T(8,128)}, f32[16,256,256]{1,2,0:T(8,128)S(1)}, u32[]{:S(2)}) copy-start(f32[16,256,256]{1,2,0:T(8,128)S(1)} %fusion.5) | copy-start | bytes 12582916
Sparse Core Ops, SparseCore 0:
  9.1 28.5 all-gather.4
  51.0 118.5 all-gather.6
where the time goes:
time: 506 us; the launch traced here: 497 us
  other arithmetic  187 us (37%)
  waiting for transfers between devices  166 us (33%)
  local copies, waits for them, and re-layouts  64.9 us (13%)
  matrix products  42.9 us (8%)
  between operations  18.4 us (4%)
  starting transfers between devices  17.2 us (3%)
    ppermute x6, waiting for transfers between devices, on_device(): lax.ppermute(share, 'col', [(i, (i + span) % n_col) for i in range(n_col)])  121 us
    another operation x20, other arithmetic, factor(): low = jnp.linalg.cholesky(tile)  104 us
    another operation x6, other arithmetic, factor(): inverse = lax.linalg.triangular_solve(low, eye, left_side=True, lower=True)  61 us
    all_gather x1, waiting for transfers between devices, on_device(): head = lax.all_gather(tiles[0], 'row', axis=0, tiled=False)  29.2 us
    dot_general x20, matrix products, mm_hi(): jnp.einsum('...ps,qs->...pq', a, b, precision=HI, preferred_element_type=...  28.1 us
    unnamed x39, local copies, waits for them, and re-layouts  17.3 us
    another operation x22, local copies, waits for them, and re-layouts, factor(): inverse = lax.linalg.triangular_solve(low, eye, left_side=True, lower=True)  15.3 us
    ppermute x3, starting transfers between devices, on_device(): lax.ppermute(share, 'row', [(i, (i + d) % n_row) for i in range(n_row)])  12.3 us
  transfers between devices with their start and end apart: 12, of which 10 were waited for; matrix products, arithmetic and copies ran while one was open for 44% of the time, Pallas kernels for 0%

commit v1 on v0

--- a/solution.py
+++ b/solution.py
@@ -41,18 +41,6 @@
 
     head = lax.all_gather(tiles[0], "row", axis=0, tiled=False)
 
-    cols = lax.dynamic_slice_in_dim(head[:STEPS], my_row * quarter, quarter, axis=2)
-    piece = jnp.swapaxes(cols, 1, 2)
-    perm = []
-    for c in range(n_col):
-        for r in range(n_row):
-            dst_col = c - c % n_row + r
-            perm.append((c * n_row + r, dst_col * n_row + c % n_row))
-    piece = lax.ppermute(piece, ("col", "row"), perm)
-
-    gathered = lax.all_gather(piece, "col", axis=1, tiled=False)
-    raw = gathered.reshape(STEPS, tile_rows, width, width)
-
     source = [(my_row + k) % STEPS for k in range(2)]
     share = jnp.stack([jnp.where(my_col == s, tiles[0], 0.0) for s in source])
     span = 1
@@ -66,6 +54,19 @@
         for d in range(1, n_row)
     ]
     shares = jnp.stack(shares)
+
+    cols = lax.dynamic_slice_in_dim(head[:STEPS], my_row * quarter, quarter, axis=2)
+    piece = jnp.swapaxes(cols, 1, 2)
+    perm = []
+    for c in range(n_col):
+        for r in range(n_row):
+            dst_col = c - c % n_row + r
+            perm.append((c * n_row + r, dst_col * n_row + c % n_row))
+    piece, shares = lax.optimization_barrier((piece, shares))
+    piece = lax.ppermute(piece, ("col", "row"), perm)
+
+    gathered = lax.all_gather(piece, "col", axis=1, tiled=False)
+    raw = gathered.reshape(STEPS, tile_rows, width, width)
 
     def lead(group, k):
         from_group = lax.dynamic_index_in_dim(shares, (my_row - group) % n_row, 0, keepdims=False)

time: 506 us -> 469 us (0.927)
  waiting for transfers between devices: 166 us -> 118 us
  starting transfers between devices: 17.2 us -> 40.3 us
  local copies, waits for them, and re-layouts: 64.9 us -> 59.4 us
    ppermute x6, waiting for transfers between devices: 121 us -> 91.4 us  [on_device(): lax.ppermute(share, 'col', [(i, (i + span) % n_col) for i in range(n_col)])]
    ppermute x1, starting transfers between devices: 4.35 us -> 26.7 us  [on_device(): piece = lax.ppermute(piece, ('col', 'row'), perm)]
    ppermute x6, starting transfers between devices: 0.51 us -> 10.6 us  [on_device(): lax.ppermute(share, 'col', [(i, (i + span) % n_col) for i in range(n_col)])]
    ppermute x3, starting transfers between devices: 12.3 us -> 3.05 us  [on_device(): lax.ppermute(share, 'row', [(i, (i + d) % n_row) for i in range(n_row)])]
    ppermute x3, waiting for transfers between devices: 8.82 us -> 0.01 us  [on_device(): lax.ppermute(share, 'row', [(i, (i + d) % n_row) for i in range(n_row)])]
    all_gather x1, waiting for transfers between devices: 29.2 us -> 21.9 us  [on_device(): head = lax.all_gather(tiles[0], 'row', axis=0, tiled=False)]
    unnamed x39 -> x33, local copies, waits for them, and re-layouts: 17.3 us -> 17 us
  transfers between devices with their start and end apart: 12 -> 12, of which waited for: 10 -> 8; matrix products, arithmetic and copies ran while one was open for 44% -> 45% of each run, Pallas kernels for 0% -> 0%
where the time goes in v1:
time: 469 us; the launch traced here: 461 us
  other arithmetic  184 us (39%)
  waiting for transfers between devices  118 us (25%)
  local copies, waits for them, and re-layouts  59.4 us (13%)
  starting transfers between devices  40.3 us (9%)
  matrix products  40.3 us (9%)
  between operations  18.3 us (4%)
    another operation x20, other arithmetic, factor(): low = jnp.linalg.cholesky(tile)  103 us
    ppermute x6, waiting for transfers between devices, on_device(): lax.ppermute(share, 'col', [(i, (i + span) % n_col) for i in range(n_col)])  91.4 us
    another operation x6, other arithmetic, factor(): inverse = lax.linalg.triangular_solve(low, eye, left_side=True, lower=True)  60.3 us
    ppermute x1, starting transfers between devices, on_device(): piece = lax.ppermute(piece, ('col', 'row'), perm)  26.7 us
    dot_general x20, matrix products, mm_hi(): jnp.einsum('...ps,qs->...pq', a, b, precision=HI, preferred_element_type=...  26.5 us
    all_gather x1, waiting for transfers between devices, on_device(): head = lax.all_gather(tiles[0], 'row', axis=0, tiled=False)  21.9 us
    unnamed x33, local copies, waits for them, and re-layouts  17 us
    another operation x22, local copies, waits for them, and re-layouts, factor(): inverse = lax.linalg.triangular_solve(low, eye, left_side=True, lower=True)  11.9 us
  transfers between devices with their start and end apart: 12, of which 8 were waited for; matrix products, arithmetic and copies ran while one was open for 45% of the time, Pallas kernels for 0%

profile of v1, /device:TPU:16, one launch (start us, length us, event | category | flops | bytes accessed | tf_op | source)
XLA Modules:
  0.0 460.9 jit_solution(13824226517614425364)
XLA Ops:
  8.1 14.2 %collective-permute-done = f32[2,256,256]{1,2,0:T(8,128)S(1)} collective-permute-done((f32[2,256,256]{1,2,0:T(8,128)S(1)}, f32[2,256,256]{1,2,0:T(8,128)S(1)}, u32[]{:S(2)}, u32[]{:S(2)}) %collective-permute-start) | collective-permute-done | bytes 524320 | tf_op jit(solution)/shard_map/ppermute | solution.py:48
  22.6 12.4 %collective-permute-done.1 = f32[2,256,256]{1,2,0:T(8,128)S(1)} collective-permute-done((f32[2,256,256]{1,2,0:T(8,128)S(1)}, f32[2,256,256]{1,2,0:T(8,128)S(1)}, u32[]{:S(2)}, u32[]{:S(2)}) %collective-permute-start.1) | collective-permute-done | bytes 524320 | tf_op jit(solution)/shard_map/ppermute | solution.py:48
  35.4 21.9 %collective-permute-done.2 = f32[2,256,256]{1,2,0:T(8,128)S(1)} collective-permute-done((f32[2,256,256]{1,2,0:T(8,128)S(1)}, f32[2,256,256]{1,2,0:T(8,128)S(1)}, u32[]{:S(2)}, u32[]{:S(2)}) %collective-permute-start.2) | collective-permute-done | bytes 524320 | tf_op jit(solution)/shard_map/ppermute | solution.py:48
  57.6 27.4 %collective-permute-done.3 = f32[2,256,256]{1,2,0:T(8,128)S(1)} collective-permute-done((f32[2,256,256]{1,2,0:T(8,128)S(1)}, f32[2,256,256]{1,2,0:T(8,128)S(1)}, u32[]{:S(2)}, u32[]{:S(2)}) %collective-permute-start.3) | collective-permute-done | bytes 524320 | tf_op jit(solution)/shard_map/ppermute | solution.py:48
  88.6 8.3 %collective-permute-done.4 = f32[2,256,256]{1,2,0:T(8,128)S(1)} collective-permute-done((f32[2,256,256]{1,2,0:T(8,128)S(1)}, f32[2,256,256]{1,2,0:T(8,128)S(1)}, u32[]{:S(2)}, u32[]{:S(2)}) %collective-permute-start.4) | collective-permute-done | bytes 524320 | tf_op jit(solution)/shard_map/ppermute | solution.py:48
  97.0 7.7 %collective-permute-start.5 = (f32[2,256,256]{1,2,0:T(8,128)S(1)}, f32[2,256,256]{1,2,0:T(8,128)S(1)}, u32[]{:S(2)}, u32[]{:S(2)}) collective-permute-start(f32[2,256,256]{1,2,0:T(8,128)S(1)} %broadcast_select_fusion.4), channel_id=1, source_target_pairs={{0,128},{4,132},{8,136},{12,140},{16,144},{20,148},{24,152},{28,15... | collective-permute-start | bytes 1572872 | tf_op jit(solution)/shard_map/ppermute | solution.py:48
  104.8 7.1 %collective-permute-done.5 = f32[2,256,256]{1,2,0:T(8,128)S(1)} collective-permute-done((f32[2,256,256]{1,2,0:T(8,128)S(1)}, f32[2,256,256]{1,2,0:T(8,128)S(1)}, u32[]{:S(2)}, u32[]{:S(2)}) %collective-permute-start.5) | collective-permute-done | bytes 524320 | tf_op jit(solution)/shard_map/ppermute | solution.py:48
  115.1 21.9 %all-gather.5.cloned.1.call-done = f32[4,1,256,1,1,256]{5,2,4,3,1,0:T(8,128)} async-done(((f32[1,1,256,1,1,256]{5,2,4,3,1,0:T(8,128)}), f32[4,1,256,1,1,256]{5,2,4,3,1,0:T(8,128)}) %all-gather.5.cloned.1.call-update) | async-done | bytes 1048592 | tf_op jit(solution)/shard_map/all_gather | solution.py:42
  141.1 26.7 %collective-permute-start.9 = (f32[3,64,256]{2,1,0:T(8,128)S(1)}, f32[3,64,256]{2,1,0:T(8,128)S(1)}, u32[]{:S(2)}, u32[]{:S(2)}) collective-permute-start(f32[3,64,256]{2,1,0:T(8,128)S(1)} %dynamic-slice_bitcast_fusion.8), channel_id=1, source_target_pairs={{0,0},{1,4},{2,8},{3,12},{4,1},{5,5},{6,9},{7,13},{8,2},{9,6},{10,... | collective-permute-start | bytes 589832 | tf_op jit(solution)/shard_map/ppermute | solution.py:66
  167.8 5.0 %collective-permute-done.9 = f32[3,64,256]{2,1,0:T(8,128)S(1)} collective-permute-done((f32[3,64,256]{2,1,0:T(8,128)S(1)}, f32[3,64,256]{2,1,0:T(8,128)S(1)}, u32[]{:S(2)}, u32[]{:S(2)}) %collective-permute-start.9) | collective-permute-done | bytes 196640 | tf_op jit(solution)/shard_map/ppermute | solution.py:66
  173.6 10.9 %copy.39 = f32[16,1,256,1,1,256]{2,5,0,4,3,1:T(8,128)} copy(f32[16,1,256,1,1,256]{5,4,3,2,1,0:T(1,128)} %param.10) | data formatting | bytes 8388608 | tf_op args[0]
  184.8 11.7 %cholesky.172 = f32[128,128]{1,0:T(8,128)S(1)} custom-call(f32[128,128]{1,0:T(8,128)S(1)} %cholesky.270), custom_call_target="Cholesky" | custom-call | tf_op jit(solution)/shard_map/jit(cholesky)/cholesky | solution.py:26
  196.6 9.8 %custom-call.15 = f32[1,128,128]{1,2,0:T(8,128)S(1)} custom-call(f32[1,128,128]{2,1,0:T(8,128)S(1)} %get-tuple-element.118), custom_call_target="InvertDiagBlocksLowerTriangular" | custom-call | tf_op jit(solution)/shard_map/jit(cholesky)/cholesky | solution.py:26
  206.9 11.7 %cholesky.189 = f32[128,128]{1,0:T(8,128)S(1)} custom-call(f32[128,128]{1,0:T(8,128)S(1)} %convolution_subtract_fusion.9), custom_call_target="Cholesky" | custom-call | tf_op jit(solution)/shard_map/jit(cholesky)/cholesky | solution.py:26
  220.7 4.1 while.9
  224.8 20.1 %custom-call.16 = f32[2,128,128]{1,2,0:T(8,128)S(1)} custom-call(f32[2,128,128]{2,1,0:T(8,128)S(1)} %get-tuple-element.67), custom_call_target="InvertDiagBlocksLowerTriangular" | custom-call | tf_op jit(solution)/shard_map/triangular_solve/custom-call.0 | solution.py:27
  247.6 11.7 %cholesky.206 = f32[128,128]{1,0:T(8,128)S(1)} custom-call(f32[128,128]{1,0:T(8,128)S(1)} %cholesky.273), custom_call_target="Cholesky" | custom-call | tf_op jit(solution)/shard_map/jit(cholesky)/cholesky | solution.py:26
  259.4 9.8 %custom-call.17 = f32[1,128,128]{1,2,0:T(8,128)S(1)} custom-call(f32[1,128,128]{2,1,0:T(8,128)S(1)} %get-tuple-element.114), custom_call_target="InvertDiagBlocksLowerTriangular" | custom-call | tf_op jit(solution)/shard_map/jit(cholesky)/cholesky | solution.py:26
  271.3 11.7 %cholesky.223 = f32[128,128]{1,0:T(8,128)S(1)} custom-call(f32[128,128]{1,0:T(8,128)S(1)} %convolution_subtract_fusion.8), custom_call_target="Cholesky" | custom-call | tf_op jit(solution)/shard_map/jit(cholesky)/cholesky | solution.py:26
  289.6 20.4 %custom-call.18 = f32[2,128,128]{1,2,0:T(8,128)} custom-call(f32[2,128,128]{2,1,0:T(8,128)S(1)} %get-tuple-element.68), custom_call_target="InvertDiagBlocksLowerTriangular" | custom-call | tf_op jit(solution)/shard_map/triangular_solve/custom-call.0 | solution.py:27
  315.2 11.7 %cholesky.240 = f32[128,128]{1,0:T(8,128)S(1)} custom-call(f32[128,128]{1,0:T(8,128)S(1)} %cholesky.276), custom_call_target="Cholesky" | custom-call | tf_op jit(solution)/shard_map/jit(cholesky)/cholesky | solution.py:26
  326.9 9.8 %custom-call.19 = f32[1,128,128]{1,2,0:T(8,128)S(1)} custom-call(f32[1,128,128]{2,1,0:T(8,128)S(1)} %get-tuple-element.110), custom_call_target="InvertDiagBlocksLowerTriangular" | custom-call | tf_op jit(solution)/shard_map/jit(cholesky)/cholesky | solution.py:26
  337.2 11.9 %cholesky.257 = f32[128,128]{1,0:T(8,128)S(1)} custom-call(f32[128,128]{1,0:T(8,128)S(1)} %convolution_subtract_fusion.7), custom_call_target="Cholesky" | custom-call | tf_op jit(solution)/shard_map/jit(cholesky)/cholesky | solution.py:26
  356.7 19.7 %custom-call.20 = f32[2,128,128]{1,2,0:T(8,128)S(1)} custom-call(f32[2,128,128]{2,1,0:T(8,128)S(1)} %get-tuple-element.69), custom_call_target="InvertDiagBlocksLowerTriangular" | custom-call | tf_op jit(solution)/shard_map/triangular_solve/custom-call.0 | solution.py:27
  381.3 9.5 %fusion.104 = (f32[1,4096,256]{2,1,0:T(8,128)}, f32[1,4096,256]{2,1,0:T(8,128)}, f32[1,4096,256]{2,1,0:T(8,128)}) fusion(f32[3,4096,256]{2,1,0:T(8,128)} %all-gather.7.cloned.1.call-done), kind=kLoop, calls=%fused_computation.205 | loop fusion | bytes 25165824 | tf_op jit(solution)/shard_map/slice | solution.py:104
  390.8 6.1 %fusion.40 = f32[16,256,256]{1,2,0:T(8,128)S(1)} fusion(f32[16,256,256]{2,1,0:T(8,128)} %bitcast.270, f32[128,256]{1,0:T(8,128)S(1)} %fusion.69, f32[128,256]{1,0:T(8,128)S(1)} %fusion.58), kind=kOutput, calls=%fused_computation.87 | convolution fusion | flops 3221291008 | bytes 8650752 | tf_op jit(solution)/shard_map/...ps,qs->...pq/dot_general | solution.py:11
  400.6 4.5 fusion.8
  408.8 4.7 %fusion.5 = f32[16,256,256]{1,2,0:T(8,128)S(1)} fusion(f32[16,256,256]{2,1,0:T(8,128)S(1)} %fusion.16, f32[16,256,256]{2,1,0:T(8,128)S(1)} %bitcast.271, f32[16,256,256]{2,1,0:T(8,128)S(1)} %fusion.18, f32[128,256]{1,0:T(8,128)S(1)} %fusion.61, f32[128,256]{1,0:T(8,128)S(1)} %fusion.54), kind=kOutput, calls=%fused_computation.14 | convolution fusion | flops 3223388160 | bytes 17039360 | tf_op jit(solution)/shard_map/...ps,qs->...pq/dot_general | solution.py:11
  413.5 5.7 %pad_maximum_fusion = f32[16,256,768]{1,2,0:T(8,128)} fusion(f32[16,256,256]{1,2,0:T(8,128)S(1)} %fusion.5, f32[16,256,256]{1,2,0:T(8,128)S(1)} %fusion.8, f32[16,256,256]{1,2,0:T(8,128)S(1)} %fusion.40), kind=kLoop, calls=%fused_computation.6 | loop fusion | flops 6291456 | bytes 25165824 | tf_op jit(solution)/shard_map/concatenate | solution.py:119
  422.8 5.3 %copy.56 = f32[16,256,256]{1,2,0:T(8,128)} copy(f32[16,256,256]{2,1,0:T(8,128)} %fusion) | data formatting | bytes 8388608 | tf_op jit(solution)/shard_map/...ps,qs->...pq/dot_general | solution.py:17
  432.5 10.4 %fusion.3 = f32[16,1,256,1,1,256]{2,5,0,4,3,1:T(8,128)} fusion(f32[16,256,256]{1,2,0:T(8,128)} %fusion.22, f32[16,1,256,1,1,256]{2,5,0,4,3,1:T(8,128)} %copy.39, f32[16,256,256]{1,2,0:T(8,128)} %copy-done, f32[16,256,256]{1,2,0:T(8,128)} %copy-done.1, f32[16,256,256]{1,2,0:T(8,128)} %copy-done.2, f32[256,256]{0,1:T(8,128)S(1)} %copy.57, ...), kind=kLoop, calls=%fused_computation.11 | loop fusion | flops 7340032 | bytes 25428020 | tf_op jit(solution)/shard_map/reshape | solution.py:137
  443.0 10.9 %copy.58 = f32[16,1,256,1,1,256]{5,4,3,2,1,0:T(1,128)} copy(f32[16,1,256,1,1,256]{2,5,0,4,3,1:T(8,128)} %fusion.3) | data formatting | bytes 8388608 | tf_op jit(solution)/shard_map/reshape | solution.py:137
  (167 shorter events, 69.4 us)
Async XLA Ops:
  6.5 130.4 %all-gather.5.cloned.1.call-start = ((), (), s32[]{:S(2)}) async-start(), calls=%async_computation | async-start | bytes 1310720 | tf_op jit(solution)/shard_map/all_gather | solution.py:42
  7.9 14.4 %collective-permute-start = (f32[2,256,256]{1,2,0:T(8,128)S(1)}, f32[2,256,256]{1,2,0:T(8,128)S(1)}, u32[]{:S(2)}, u32[]{:S(2)}) collective-permute-start(f32[2,256,256]{1,2,0:T(8,128)S(1)} %pad_maximum_fusion.4), channel_id=1, source_target_pairs={{0,4},{4,8},{8,12},{12,16},{16,20},{20,24},{24,28},{28,32},{32,36}... | collective-permute-start | bytes 1572872 | tf_op jit(solution)/shard_map/ppermute | solution.py:48
  22.5 12.6 %collective-permute-start.1 = (f32[2,256,256]{1,2,0:T(8,128)S(1)}, f32[2,256,256]{1,2,0:T(8,128)S(1)}, u32[]{:S(2)}, u32[]{:S(2)}) collective-permute-start(f32[2,256,256]{1,2,0:T(8,128)S(1)} %broadcast_select_fusion), channel_id=1, source_target_pairs={{0,8},{4,12},{8,16},{12,20},{16,24},{20,28},{24,32},{28,36},{32,40... | collective-permute-start | bytes 1572872 | tf_op jit(solution)/shard_map/ppermute | solution.py:48
  35.2 22.1 %collective-permute-start.2 = (f32[2,256,256]{1,2,0:T(8,128)S(1)}, f32[2,256,256]{1,2,0:T(8,128)S(1)}, u32[]{:S(2)}, u32[]{:S(2)}) collective-permute-start(f32[2,256,256]{1,2,0:T(8,128)S(1)} %broadcast_select_fusion.1), channel_id=1, source_target_pairs={{0,16},{4,20},{8,24},{12,28},{16,32},{20,36},{24,40},{28,44},{32,4... | collective-permute-start | bytes 1572872 | tf_op jit(solution)/shard_map/ppermute | solution.py:48
  57.4 27.6 %collective-permute-start.3 = (f32[2,256,256]{1,2,0:T(8,128)S(1)}, f32[2,256,256]{1,2,0:T(8,128)S(1)}, u32[]{:S(2)}, u32[]{:S(2)}) collective-permute-start(f32[2,256,256]{1,2,0:T(8,128)S(1)} %broadcast_select_fusion.2), channel_id=1, source_target_pairs={{0,32},{4,36},{8,40},{12,44},{16,48},{20,52},{24,56},{28,60},{32,6... | collective-permute-start | bytes 1572872 | tf_op jit(solution)/shard_map/ppermute | solution.py:48
  85.2 11.7 %collective-permute-start.4 = (f32[2,256,256]{1,2,0:T(8,128)S(1)}, f32[2,256,256]{1,2,0:T(8,128)S(1)}, u32[]{:S(2)}, u32[]{:S(2)}) collective-permute-start(f32[2,256,256]{1,2,0:T(8,128)S(1)} %broadcast_select_fusion.3), channel_id=1, source_target_pairs={{0,64},{4,68},{8,72},{12,76},{16,80},{20,84},{24,88},{28,92},{32,9... | collective-permute-start | bytes 1572872 | tf_op jit(solution)/shard_map/ppermute | solution.py:48
  88.5 292.8 %all-gather.7.cloned.1.call-start = ((), (), s32[]{:S(2)}) async-start(), calls=%async_computation.1 | async-start | bytes 12779520 | tf_op jit(solution)/shard_map/all_gather | solution.py:68
  97.0 14.9 %collective-permute-start.5 = (f32[2,256,256]{1,2,0:T(8,128)S(1)}, f32[2,256,256]{1,2,0:T(8,128)S(1)}, u32[]{:S(2)}, u32[]{:S(2)}) collective-permute-start(f32[2,256,256]{1,2,0:T(8,128)S(1)} %broadcast_select_fusion.4), channel_id=1, source_target_pairs={{0,128},{4,132},{8,136},{12,140},{16,144},{20,148},{24,152},{28,15... | collective-permute-start | bytes 1572872 | tf_op jit(solution)/shard_map/ppermute | solution.py:48
  112.0 26.4 %collective-permute-start.6 = (f32[2,256,256]{1,2,0:T(8,128)S(1)}, f32[2,256,256]{1,2,0:T(8,128)S(1)}, u32[]{:S(2)}, u32[]{:S(2)}) collective-permute-start(f32[2,256,256]{1,2,0:T(8,128)S(1)} %broadcast_select_fusion.5), channel_id=1, source_target_pairs={{0,1},{1,2},{2,3},{3,0},{4,5},{5,6},{6,7},{7,4},{8,9},{9,10},{10,1... | collective-permute-start | bytes 1572872 | tf_op jit(solution)/shard_map/ppermute | solution.py:53
  113.4 25.1 %collective-permute-start.7 = (f32[2,256,256]{1,2,0:T(8,128)S(1)}, f32[2,256,256]{1,2,0:T(8,128)S(1)}, u32[]{:S(2)}, u32[]{:S(2)}) collective-permute-start(f32[2,256,256]{1,2,0:T(8,128)S(1)} %broadcast_select_fusion.5), channel_id=1, source_target_pairs={{0,2},{1,3},{2,0},{3,1},{4,6},{5,7},{6,4},{7,5},{8,10},{9,11},{10,... | collective-permute-start | bytes 1572872 | tf_op jit(solution)/shard_map/ppermute | solution.py:53
  114.0 24.5 %collective-permute-start.8 = (f32[2,256,256]{1,2,0:T(8,128)S(1)}, f32[2,256,256]{1,2,0:T(8,128)}, u32[]{:S(2)}, u32[]{:S(2)}) collective-permute-start(f32[2,256,256]{1,2,0:T(8,128)S(1)} %broadcast_select_fusion.5), channel_id=1, source_target_pairs={{0,3},{1,0},{2,1},{3,2},{4,7},{5,4},{6,5},{7,6},{8,11},{9,8},{10,9... | collective-permute-start | bytes 1572872 | tf_op jit(solution)/shard_map/ppermute | solution.py:53
  138.4 46.1 %copy-start.5 = (f32[3,1,256,1,1,256]{2,5,0,4,3,1:T(8,128)}, f32[3,1,256,1,1,256]{2,5,0,4,3,1:T(8,128)S(1)}, u32[]{:S(2)}) copy-start(f32[3,1,256,1,1,256]{2,5,0,4,3,1:T(8,128)S(1)} %copy.70) | copy-start | bytes 2359300
  138.5 0.9 copy-start.12
  138.5 1.0 copy-start.13
  141.1 31.7 %collective-permute-start.9 = (f32[3,64,256]{2,1,0:T(8,128)S(1)}, f32[3,64,256]{2,1,0:T(8,128)S(1)}, u32[]{:S(2)}, u32[]{:S(2)}) collective-permute-start(f32[3,64,256]{2,1,0:T(8,128)S(1)} %dynamic-slice_bitcast_fusion.8), channel_id=1, source_target_pairs={{0,0},{1,4},{2,8},{3,12},{4,1},{5,5},{6,9},{7,13},{8,2},{9,6},{10,... | collective-permute-start | bytes 589832 | tf_op jit(solution)/shard_map/ppermute | solution.py:66
  172.8 0.7 copy-start.14
  218.6 26.9 %copy-start.7 = (f32[256,256]{1,0:T(8,128)}, f32[256,256]{1,0:T(8,128)S(1)}, u32[]{:S(2)}) copy-start(f32[256,256]{1,0:T(8,128)S(1)} %get-tuple-element.116) | copy-start | bytes 786436
  246.9 0.7 copy-start.11
  283.1 6.5 %copy-start.8 = (f32[256,256]{1,0:T(8,128)}, f32[256,256]{1,0:T(8,128)S(1)}, u32[]{:S(2)}) copy-start(f32[256,256]{1,0:T(8,128)S(1)} %get-tuple-element.112) | copy-start | bytes 786436
  313.2 1.3 copy-start.9
  314.5 62.9 %copy-start.6 = (f32[3,1,256,1,1,256]{2,5,0,4,3,1:T(8,128)S(1)}, f32[3,1,256,1,1,256]{2,5,0,4,3,1:T(8,128)}, u32[]{:S(2)}) copy-start(f32[3,1,256,1,1,256]{2,5,0,4,3,1:T(8,128)} %copy-done.5) | copy-start | bytes 2359300
  315.1 63.6 %copy-start.10 = (f32[128,256]{1,0:T(8,128)S(1)}, f32[128,256]{1,0:T(8,128)}, u32[]{:S(2)}) copy-start(f32[128,256]{1,0:T(8,128)} %copy-done.9) | copy-start | bytes 393220
  396.9 22.3 %copy-start = (f32[16,256,256]{1,2,0:T(8,128)}, f32[16,256,256]{1,2,0:T(8,128)S(1)}, u32[]{:S(2)}) copy-start(f32[16,256,256]{1,2,0:T(8,128)S(1)} %fusion.40) | copy-start | bytes 12582916
  397.7 2.9 copy-start.3
  405.0 14.1 %copy-start.1 = (f32[16,256,256]{1,2,0:T(8,128)}, f32[16,256,256]{1,2,0:T(8,128)S(1)}, u32[]{:S(2)}) copy-start(f32[16,256,256]{1,2,0:T(8,128)S(1)} %fusion.8) | copy-start | bytes 12582916
  405.1 3.7 copy-start.4
  413.5 5.8 %copy-start.2 = (f32[16,256,256]{1,2,0:T(8,128)}, f32[16,256,256]{1,2,0:T(8,128)S(1)}, u32[]{:S(2)}) copy-start(f32[16,256,256]{1,2,0:T(8,128)S(1)} %fusion.5) | copy-start | bytes 12582916
Sparse Core Ops, SparseCore 0:
  88.6 48.3 all-gather.4
  173.6 84.6 all-gather.6
